TPU v7x, 256 devices: a whole 4x4x8 slice. The times are simulated.
256 devices in a mesh: seq: 32 (over x, z), tensor: 8 (over y, core).
Axes of the slice: x: 4, y: 4, z: 8, core: 2. Of those that a mesh axis runs over, the one named last changes fastest.
Arguments:
- queries: bfloat16 [10240, 4096], P('seq', 'tensor'), may hold values from -8 to 8
- key_rows: bfloat16 [10240, 1024], P('seq', 'tensor'), may hold values from -8 to 8
- value_rows: bfloat16 [10240, 1024], P('seq', 'tensor'), may hold values from -6 to 6
- out_weight: bfloat16 [4096, 8192], P('tensor', 'seq'), may hold values from -0.09375 to 0.09375
- residual_in: bfloat16 [10240, 8192], P('seq'), may hold values from -0.1796875 to 0.1796875
- norm_gain: bfloat16 [8192], replicated, may hold values from 0.099609375 to 1.8984375
- prompt_lengths: int32 [18], replicated, may hold values from 1 to 5120, 10240 in all
Outputs:
- normed: bfloat16 [10240, 8192], P('seq')
- cache_keys: bfloat16 [22528, 1024], P('seq', 'tensor')
- cache_values: bfloat16 [22528, 1024], P('seq', 'tensor')
Inputs may be any that keep to these rules, and one draw needn't show every extreme that they name: `prompt_lengths`: the 18 lengths sum to 10240, and the largest is 5120.
All inputs are finite; a program needn't handle non-finite values.
Results may differ from a plain program's by a relative error of at most 0.019.
Values may be sent and summed in bfloat16 or wider, within the bound.
No kernel may reach another device: no remote copies, remote signals or barrier semaphores. Data moves between devices by JAX's collectives and lax.ppermute only.
A program may use at most 192 MiB of HBM per device.

v0:
```python
import math
import jax
import jax.numpy as jnp
from jax import lax
from jax.sharding import PartitionSpec as P

HD = 128
PAGE = 128
SLOT_DEV = 704


def position_of(stored, per_device, devices):
    half_block = per_device // 2
    device = stored // per_device
    offset = stored % per_device
    return jnp.where(
        offset < half_block,
        device * half_block + offset,
        (2 * devices - 1 - device) * half_block + offset - half_block,
    )


def stored_row(position, per_device, devices):
    half_block = per_device // 2
    block_index = position // half_block
    device = jnp.where(block_index < devices, block_index, 2 * devices - 1 - block_index)
    offset = position % half_block + jnp.where(block_index < devices, 0, half_block)
    return device * per_device + offset


def segment_of(position, lengths):
    doc_ends = jnp.cumsum(lengths, dtype=jnp.int32)
    return jnp.sum(
        (position[:, None] >= doc_ends[None, :]).astype(jnp.int32), axis=1, dtype=jnp.int32
    )


def slot_source(slot_ids, lengths, page_size):
    padded = (lengths + page_size - 1) // page_size * page_size
    page_ends = jnp.cumsum(padded, dtype=jnp.int32)
    page_starts = page_ends - padded
    doc_ends = jnp.cumsum(lengths, dtype=jnp.int32)
    doc_starts = doc_ends - lengths
    before = (slot_ids[:, None] >= page_ends[None, :]).astype(jnp.int32)
    inside = (slot_ids[:, None] >= page_starts[None, :]).astype(jnp.int32) - before
    page_start = jnp.sum(before * padded[None, :], axis=1, dtype=jnp.int32)
    doc_start = jnp.sum(before * lengths[None, :], axis=1, dtype=jnp.int32)
    length = jnp.sum(inside * lengths[None, :], axis=1, dtype=jnp.int32)
    within = slot_ids - page_start
    is_live = within < length
    return (doc_start + within, is_live)


def body(queries, key_rows, value_rows, out_weight, residual_in, norm_gain, prompt_lengths):
    seq_count = lax.axis_size("seq")
    seq_index = lax.axis_index("seq")
    per_device = queries.shape[0]
    kv_local = key_rows.shape[1] // HD
    group_size = queries.shape[1] // (kv_local * HD)
    score_scale = 1.0 / math.sqrt(HD)
    local_rows = jnp.arange(per_device, dtype=jnp.int32) + seq_index * per_device
    my_position = position_of(local_rows, per_device, seq_count)
    my_segment = segment_of(my_position, prompt_lengths)
    grouped = queries.reshape(per_device, kv_local, group_size, HD)
    kv_width = key_rows.shape[1]
    kv_piece = lax.all_gather(
        jnp.concatenate([key_rows, value_rows], axis=1), "seq", axis=0, tiled=True
    )
    key_piece = kv_piece[:, :kv_width]
    value_piece = kv_piece[:, kv_width:]
    piece_rows = key_piece.shape[0]
    key_position = position_of(jnp.arange(piece_rows, dtype=jnp.int32), per_device, seq_count)
    key_segment = segment_of(key_position, prompt_lengths)
    allowed = (key_position[None, :] <= my_position[:, None]) & (
        key_segment[None, :] == my_segment[:, None]
    )
    top_old = jnp.full((kv_local, group_size, per_device), -1e30, jnp.float32)
    scores = (
        jnp.einsum(
            "qgjd,kgd->gjqk",
            grouped,
            key_piece.reshape(piece_rows, kv_local, HD),
            preferred_element_type=jnp.float32,
        )
        * score_scale
    )
    scores = jnp.where(allowed, scores, -1e30)
    top_new = jnp.maximum(top_old, jnp.max(scores, axis=-1))
    weights = jnp.where(allowed, jnp.exp(scores - top_new[..., None]), 0.0)
    total_new = jnp.sum(weights, axis=-1)
    accum_new = jnp.einsum(
        "gjqk,kgd->gjqd",
        weights.astype(jnp.bfloat16),
        value_piece.reshape(piece_rows, kv_local, HD),
        preferred_element_type=jnp.float32,
    )
    attended = jnp.transpose(accum_new / total_new[..., None], (2, 0, 1, 3))
    attended = attended.reshape(per_device, -1).astype(jnp.bfloat16)
    partial_value = jnp.dot(
        attended,
        lax.all_gather(out_weight, "seq", axis=1, tiled=True),
        preferred_element_type=jnp.float32,
    )
    projected = lax.psum(partial_value.astype(jnp.bfloat16), "tensor").astype(jnp.float32)
    hidden = residual_in.astype(jnp.float32) + projected
    mean_square = jnp.mean(hidden * hidden, axis=-1, keepdims=True)
    normed = (hidden * lax.rsqrt(mean_square + 1e-05) * norm_gain.astype(jnp.float32)).astype(
        jnp.bfloat16
    )
    slot_ids = seq_index * SLOT_DEV + jnp.arange(SLOT_DEV, dtype=jnp.int32)
    source, is_live = slot_source(slot_ids, prompt_lengths, PAGE)
    target = stored_row(source, per_device, seq_count)
    empty_cache = jnp.zeros((SLOT_DEV, kv_local * HD), jnp.bfloat16)
    found = is_live & (target >= 0) & (target < piece_rows)
    safe_index = jnp.clip(target, 0, piece_rows - 1)
    cache_keys = jnp.where(found[:, None], jnp.take(key_piece, safe_index, axis=0), empty_cache)
    cache_values = jnp.where(found[:, None], jnp.take(value_piece, safe_index, axis=0), empty_cache)
    return (normed, cache_keys, cache_values)


def solution(mesh):
    return jax.shard_map(
        body,
        mesh=mesh,
        in_specs=(
            P("seq", "tensor"),
            P("seq", "tensor"),
            P("seq", "tensor"),
            P("tensor", "seq"),
            P("seq", None),
            P(),
            P(),
        ),
        out_specs=(P("seq", None), P("seq", "tensor"), P("seq", "tensor")),
        check_vma=False,
    )
```

profile of v0, /device:TPU:1, one launch (start us, length us, event | category | flops | bytes accessed | tf_op | source)
XLA Modules:
  0.0 310.1 jit_solution(13555092218789178911)
XLA Ops:
  7.2 0.0 all-gather.3.cloned.1.call-start
  7.2 1.6 pad_maximum_fusion
  8.9 0.0 all-gather.3.cloned.1.call-update
  8.9 0.0 all-gather.5.cloned.1.call-start
  9.0 0.7 all-gather.5.cloned.1.call-update
  9.7 0.0 all-reduce.2.cloned.1.call-start
  9.7 0.7 copy.17
  10.5 0.1 reduce.2
  10.6 0.7 convert_element_type.52
  11.3 0.7 fusion.65
  12.0 0.1 copy.20
  12.1 0.1 reduce.3
  12.3 0.7 fusion.55
  13.0 0.7 fusion.64
  13.6 0.8 fusion.36
  14.5 0.1 convert_reduce_fusion.1
  14.6 0.2 convert_reduce_fusion
  14.8 4.6 %compare_and_fusion = pred[320,10240]{1,0:T(8,128)(4,1)} fusion(s32[10240]{0:T(1024)S(1)} %convert_reduce_fusion, s32[10240]{0:T(1024)S(1)} %fusion.43, s32[320]{0:T(512)S(1)} %convert_reduce_fusion.1, s32[320]{0:T(512)S(1)} %add_select_fusion.5), kind=kLoop, calls=%fused_computation.10 | loop fusion | flops 9830400 | bytes 3361280 | tf_op jit(solution)/shard_map/and | solution.py:74
  19.4 78.3 %all-gather.3.cloned.1.call-done = bf16[10240,256]{1,0:T(8,128)(2,1)} async-done(((bf16[320,256]{1,0:T(8,128)(2,1)}), bf16[10240,256]{1,0:T(8,128)(2,1)}) %all-gather.3.cloned.1.call-update) | async-done | bytes 5242896 | tf_op jit(solution)/shard_map/all_gather | solution.py:66
  97.7 22.9 %fusion = (f32[4,320]{1,0:T(4,128)S(1)}, f32[10240,320,4]{0,1,2:T(8,128)}) fusion(pred[320,10240]{1,0:T(8,128)(4,1)} %compare_and_fusion, bf16[10240,256]{1,0:T(8,128)(2,1)} %all-gather.3.cloned.1.call-done, bf16[320,512]{1,0:T(8,128)(2,1)S(1)} %copy-done), kind=kOutput, calls=%fused_computation.4 | convolution fusion | flops 3394763520 | bytes 58659840 | tf_op jit(solution)/shard_map/qgjd,kgd->gjqk/dot_general | solution.py:79
  120.5 22.7 %fusion.1 = f32[4,320]{1,0:T(4,128)S(1)} fusion(f32[10240,320,4]{0,1,2:T(8,128)} %get-tuple-element.14, f32[4,320]{1,0:T(4,128)S(1)} %broadcast_maximum_fusion, pred[320,10240]{1,0:T(8,128)(4,1)} %compare_and_fusion), kind=kLoop, calls=%fused_computation.5 | loop fusion | flops 65534720 | bytes 55715840 | tf_op jit(solution)/shard_map/reduce_sum | solution.py:90
  143.3 23.2 %fusion.20 = bf16[320,1,4,128]{3,0,2,1:T(8,128)(2,1)S(1)} fusion(f32[10240,320,4]{0,1,2:T(8,128)} %get-tuple-element.14, f32[4,320]{1,0:T(4,128)S(1)} %broadcast_maximum_fusion, pred[320,10240]{1,0:T(8,128)(4,1)} %compare_and_fusion, f32[4,320]{1,0:T(4,128)S(1)} %fusion.1, bf16[10240,256]{1,0:T(8,128)(2,1)} %all-gather.3.cloned.1.call-done), kind=kOutput, calls=%fused_computation.20 | convolution fusion | flops 3421306880 | bytes 58664960 | tf_op jit(solution)/shard_map/gjqk,kgd->gjqd/dot_general | solution.py:91
  166.5 0.3 copy.19
  166.8 34.2 %all-gather.5.cloned.1.call-done = bf16[512,8192]{1,0:T(8,128)(2,1)} async-done(((bf16[512,256]{1,0:T(8,128)(2,1)}), bf16[512,8192]{1,0:T(8,128)(2,1)}) %all-gather.5.cloned.1.call-update) | async-done | bytes 8388624 | tf_op jit(solution)/shard_map/all_gather | solution.py:101
  200.9 8.0 %convolution_convert_fusion = bf16[320,8192]{1,0:T(8,128)(2,1)} fusion(bf16[512,8192]{1,0:T(8,128)(2,1)} %all-gather.5.cloned.1.call-done, bf16[40,8,4,128]{3,2,1,0:T(4,128)(2,1)S(1)} %bitcast.67), kind=kOutput, calls=%fused_computation.11 | convolution fusion | flops 2686976000 | bytes 13959168 | tf_op jit(solution)/shard_map/dot_general | solution.py:99
  208.9 3.7 %fusion.62 = (bf16[10240,128]{1,0:T(8,128)(2,1)S(1)}, bf16[10240,128]{1,0:T(8,128)(2,1)}) fusion(bf16[10240,256]{1,0:T(8,128)(2,1)} %all-gather.3.cloned.1.call-done), kind=kLoop, calls=%fused_computation.91 | loop fusion | bytes 10485760 | tf_op jit(solution)/shard_map/slice | solution.py:70
  212.6 3.8 %gather_fusion = bf16[704,128]{1,0:T(8,128)(2,1)S(1)} fusion(bf16[10240,128]{1,0:T(8,128)(2,1)} %get-tuple-element.10, s32[1024]{0:T(1024)S(1)} %pad_clamp_fusion), kind=kCustom, calls=%fused_computation.clone | custom fusion | bytes 363264 | tf_op jit(solution)/shard_map/jit(_take)/gather | solution.py:116
  216.5 2.0 gather_fusion.1
  218.5 1.0 select_select_fusion
  219.5 71.0 %all-reduce.2.cloned.1.call-done = bf16[320,8192]{1,0:T(8,128)(2,1)} async-done(((bf16[320,8192]{1,0:T(8,128)(2,1)}), bf16[320,8192]{1,0:T(8,128)(2,1)}) %all-reduce.2.cloned.1.call-update) | async-done | bytes 5242896 | tf_op jit(solution)/shard_map/psum | solution.py:104
  290.5 6.0 %multiply_reduce_fusion = f32[320]{0:T(512)S(1)} fusion(bf16[320,8192]{1,0:T(8,128)(2,1)} %all-reduce.2.cloned.1.call-done, bf16[320,8192]{1,0:T(8,128)(2,1)} %param.13), kind=kLoop, calls=%fused_computation.13 | loop fusion | flops 13106880 | bytes 10487040 | tf_op jit(solution)/shard_map/reduce_sum | solution.py:106
  296.5 7.1 %multiply_convert_fusion = bf16[320,8192]{1,0:T(8,128)(2,1)} fusion(bf16[320,8192]{1,0:T(8,128)(2,1)S(1)} %copy-done.2, bf16[320,8192]{1,0:T(8,128)(2,1)} %param.13, f32[8192]{0:T(1024)S(1)} %convert_element_type.52, f32[320]{0:T(512)S(1)} %add_rsqrt_fusion), kind=kLoop, calls=%fused_computation.12 | loop fusion | flops 15728640 | bytes 15762688 | tf_op jit(solution)/shard_map/convert_element_type | solution.py:107
  (18 shorter events, 0.2 us)
Async XLA Ops:
  7.2 90.5 %copy-start = (bf16[320,512]{1,0:T(8,128)(2,1)S(1)}, bf16[320,512]{1,0:T(8,128)(2,1)}, u32[]{:S(2)}) copy-start(bf16[320,512]{1,0:T(8,128)(2,1)} %param.9) | copy-start | bytes 983044
  7.2 90.5 %all-gather.3.cloned.1.call-start = ((), (), s32[]{:S(2)}) async-start(), calls=%async_computation | async-start | bytes 5406720 | tf_op jit(solution)/shard_map/all_gather | solution.py:66
  8.9 192.0 %all-gather.5.cloned.1.call-start = ((), (), s32[]{:S(2)}) async-start(), calls=%async_computation.1 | async-start | bytes 8650752 | tf_op jit(solution)/shard_map/all_gather | solution.py:101
  9.7 280.8 %all-reduce.2.cloned.1.call-start = ((), (), s32[]{:S(2)}) async-start(), calls=%async_computation.2 | async-start | bytes 10485760 | tf_op jit(solution)/shard_map/psum | solution.py:104
  290.5 6.0 %copy-start.2 = (bf16[320,8192]{1,0:T(8,128)(2,1)S(1)}, bf16[320,8192]{1,0:T(8,128)(2,1)}, u32[]{:S(2)}) copy-start(bf16[320,8192]{1,0:T(8,128)(2,1)} %all-reduce.2.cloned.1.call-done) | copy-start | bytes 15728644
  290.5 13.1 %copy-start.1 = (bf16[320,512]{1,0:T(8,128)(2,1)S(1)}, bf16[320,512]{1,0:T(8,128)(2,1)}, u32[]{:S(2)}) copy-start(bf16[320,512]{1,0:T(8,128)(2,1)} %param.9) | copy-start | bytes 983044
Sparse Core Ops, SparseCore 0:
  11.2 86.4 all-gather.2
  100.1 100.7 all-gather.4
  209.0 81.3 all-reduce.1
where the time goes:
time: 310 us
  waiting for transfers between devices  184 us (59%)
  matrix products  54.1 us (17%)
  other arithmetic  47.3 us (15%)
  between operations  13.9 us (4%)
  local copies, waits for them, and re-layouts  10.7 us (3%)
    all_gather x1, waiting for transfers between devices, body(): lax.all_gather(jnp.concatenate([key_rows, value_rows], axis=1), 'seq', ax...  78.3 us
    psum x1, waiting for transfers between devices, body(): lax.psum(partial_value.astype(jnp.bfloat16), 'tensor').astype(jnp.float32)  71 us
    all_gather x1, waiting for transfers between devices, body(): lax.all_gather(out_weight, 'seq', axis=1, tiled=True)  34.2 us
    dot_general x1, matrix products, body(): jnp.einsum('gjqk,kgd->gjqd', weights.astype(jnp.bfloat16), value_piece.re...  23.2 us
    dot_general x1, matrix products, body(): jnp.einsum('qgjd,kgd->gjqk', grouped, key_piece.reshape(piece_rows, kv_lo...  22.9 us
    reduce_sum x1, other arithmetic, body(): total_new = jnp.sum(weights, axis=-1)  22.7 us
    dot_general x1, matrix products, body(): jnp.dot(attended, lax.all_gather(out_weight, 'seq', axis=1, tiled=True),...  7.96 us
    convert_element_type x1, other arithmetic, body(): (hidden * lax.rsqrt(mean_square + 1e-05) * norm_gain.astype(jnp.float32))...  7.13 us
  transfers between devices with their start and end apart: 3, of which 3 were waited for; matrix products, arithmetic and copies ran while one was open for 29% of the time, Pallas kernels for 0%

commit v1 on v0

--- a/solution.py
+++ b/solution.py
@@ -63,8 +63,14 @@
     my_segment = segment_of(my_position, prompt_lengths)
     grouped = queries.reshape(per_device, kv_local, group_size, HD)
     kv_width = key_rows.shape[1]
-    kv_piece = lax.all_gather(
-        jnp.concatenate([key_rows, value_rows], axis=1), "seq", axis=0, tiled=True
+    kv_piece = jnp.concatenate(
+        lax.all_to_all(
+            jnp.stack([jnp.concatenate([key_rows, value_rows], axis=1)] * lax.axis_size("seq")),
+            "seq",
+            0,
+            0,
+        ),
+        axis=0,
     )
     key_piece = kv_piece[:, :kv_width]
     value_piece = kv_piece[:, kv_width:]

time: 310 us -> 339 us (1.094)
  waiting for transfers between devices: 184 us -> 202 us
  starting transfers between devices: 0.12 us -> 12.1 us
  other arithmetic: 47.3 us -> 43.3 us
    all_to_all x0 -> x1, waiting for transfers between devices: none -> 123 us  [body(): lax.all_to_all(jnp.stack([jnp.concatenate([key_rows, value_rows], axis=1)...]
    all_gather x1 -> x0, waiting for transfers between devices: 78.3 us -> none  [body(): lax.all_gather(jnp.concatenate([key_rows, value_rows], axis=1), 'seq', ax...]
    all_gather x1, waiting for transfers between devices: 34.2 us -> 0.02 us  [body(): lax.all_gather(out_weight, 'seq', axis=1, tiled=True)]
    all_to_all x0 -> x1, starting transfers between devices: none -> 12 us  [body(): lax.all_to_all(jnp.stack([jnp.concatenate([key_rows, value_rows], axis=1)...]
    psum x1, waiting for transfers between devices: 71 us -> 77.8 us  [body(): lax.psum(partial_value.astype(jnp.bfloat16), 'tensor').astype(jnp.float32)]
  transfers between devices with their start and end apart: 3 -> 3, of which waited for: 3 -> 2; matrix products, arithmetic and copies ran while one was open for 29% -> 25% of each run, Pallas kernels for 0% -> 0%
where the time goes in v1:
time: 339 us
  waiting for transfers between devices  202 us (60%)
  matrix products  54.7 us (16%)
  other arithmetic  43.3 us (13%)
  between operations  14.2 us (4%)
  local copies, waits for them, and re-layouts  13 us (4%)
  starting transfers between devices  12.1 us (4%)
    all_to_all x1, waiting for transfers between devices, body(): lax.all_to_all(jnp.stack([jnp.concatenate([key_rows, value_rows], axis=1)...  123 us
    psum x1, waiting for transfers between devices, body(): lax.psum(partial_value.astype(jnp.bfloat16), 'tensor').astype(jnp.float32)  77.8 us
    dot_general x1, matrix products, body(): jnp.einsum('qgjd,kgd->gjqk', grouped, key_piece.reshape(piece_rows, kv_lo...  23.4 us
    dot_general x1, matrix products, body(): jnp.einsum('gjqk,kgd->gjqd', weights.astype(jnp.bfloat16), value_piece.re...  23.1 us
    reduce_sum x1, other arithmetic, body(): total_new = jnp.sum(weights, axis=-1)  22.8 us
    all_to_all x1, starting transfers between devices, body(): lax.all_to_all(jnp.stack([jnp.concatenate([key_rows, value_rows], axis=1)...  12 us
    dot_general x1, matrix products, body(): jnp.dot(attended, lax.all_gather(out_weight, 'seq', axis=1, tiled=True),...  8.21 us
    convert_element_type x1, other arithmetic, body(): (hidden * lax.rsqrt(mean_square + 1e-05) * norm_gain.astype(jnp.float32))...  7.13 us
  transfers between devices with their start and end apart: 3, of which 2 were waited for; matrix products, arithmetic and copies ran while one was open for 25% of the time, Pallas kernels for 0%

profile of v1, /device:TPU:1, one launch (start us, length us, event | category | flops | bytes accessed | tf_op | source)
XLA Modules:
  0.0 339.1 jit_solution(2640158884365046821)
XLA Ops:
  7.2 0.0 copy-start
  7.2 1.0 pad_maximum_fusion
  8.2 2.9 stack.2
  11.1 12.0 %all-to-all-start = ((bf16[32,320,256]{2,1,0:T(8,128)(2,1)}), bf16[32,320,256]{2,1,0:T(8,128)(2,1)}, u32[]{:S(2)}, u32[]{:S(2)}) async-start(bf16[32,320,256]{2,1,0:T(8,128)(2,1)} %stack.2), calls=%async_computation | async-start | bytes 10485760 | tf_op jit(solution)/shard_map/all_to_all | solution.py:67
  23.1 0.0 all-gather.2.cloned.1.call-start
  23.2 0.7 all-gather.2.cloned.1.call-update
  23.9 0.0 all-reduce.2.cloned.1.call-start
  23.9 0.1 copy.17
  24.1 0.1 reduce.2
  24.2 0.1 copy.20
  24.4 0.1 reduce.3
  24.5 0.1 fusion.36
  24.7 0.1 convert_reduce_fusion.1
  24.9 0.2 convert_reduce_fusion
  25.1 4.5 %compare_and_fusion = pred[320,10240]{1,0:T(8,128)(4,1)} fusion(s32[10240]{0:T(1024)S(1)} %convert_reduce_fusion, s32[10240]{0:T(1024)S(1)} %fusion.43, s32[320]{0:T(512)S(1)} %convert_reduce_fusion.1, s32[320]{0:T(512)S(1)} %add_select_fusion.5), kind=kLoop, calls=%fused_computation.10 | loop fusion | flops 9830400 | bytes 3361280 | tf_op jit(solution)/shard_map/and | solution.py:80
  29.7 123.2 %all-to-all-done = bf16[32,320,256]{2,1,0:T(8,128)(2,1)} async-done(((bf16[32,320,256]{2,1,0:T(8,128)(2,1)}), bf16[32,320,256]{2,1,0:T(8,128)(2,1)}, u32[]{:S(2)}, u32[]{:S(2)}) %all-to-all-start) | async-done | bytes 5242912 | tf_op jit(solution)/shard_map/all_to_all | solution.py:67
  152.9 0.0 copy-done
  152.9 23.4 %fusion = (f32[4,320]{1,0:T(4,128)S(1)}, f32[10240,320,4]{0,1,2:T(8,128)}) fusion(pred[320,10240]{1,0:T(8,128)(4,1)} %compare_and_fusion, bf16[10240,256]{1,0:T(8,128)(2,1)} %bitcast.1, bf16[320,512]{1,0:T(8,128)(2,1)S(1)} %copy-done), kind=kOutput, calls=%fused_computation.4 | convolution fusion | flops 3394763520 | bytes 58659840 | tf_op jit(solution)/shard_map/qgjd,kgd->gjqk/dot_general | solution.py:85
  176.3 22.8 %fusion.1 = f32[4,320]{1,0:T(4,128)S(1)} fusion(f32[10240,320,4]{0,1,2:T(8,128)} %get-tuple-element.14, f32[4,320]{1,0:T(4,128)S(1)} %broadcast_maximum_fusion, pred[320,10240]{1,0:T(8,128)(4,1)} %compare_and_fusion), kind=kLoop, calls=%fused_computation.5 | loop fusion | flops 65534720 | bytes 55715840 | tf_op jit(solution)/shard_map/reduce_sum | solution.py:96
  199.1 23.1 %fusion.20 = bf16[320,1,4,128]{3,0,2,1:T(8,128)(2,1)S(1)} fusion(f32[10240,320,4]{0,1,2:T(8,128)} %get-tuple-element.14, f32[4,320]{1,0:T(4,128)S(1)} %broadcast_maximum_fusion, pred[320,10240]{1,0:T(8,128)(4,1)} %compare_and_fusion, f32[4,320]{1,0:T(4,128)S(1)} %fusion.1, bf16[10240,256]{1,0:T(8,128)(2,1)} %bitcast.1), kind=kOutput, calls=%fused_computation.20 | convolution fusion | flops 3421306880 | bytes 58664960 | tf_op jit(solution)/shard_map/gjqk,kgd->gjqd/dot_general | solution.py:97
  222.2 0.3 copy.19
  222.5 0.0 all-gather.2.cloned.1.call-done
  222.5 8.2 %convolution_convert_fusion = bf16[320,8192]{1,0:T(8,128)(2,1)} fusion(bf16[512,8192]{1,0:T(8,128)(2,1)} %all-gather.2.cloned.1.call-done, bf16[40,8,4,128]{3,2,1,0:T(4,128)(2,1)S(1)} %bitcast.68), kind=kOutput, calls=%fused_computation.11 | convolution fusion | flops 2686976000 | bytes 13959168 | tf_op jit(solution)/shard_map/dot_general | solution.py:105
  230.7 0.0 all-reduce.2.cloned.1.call-update
  230.7 3.7 %fusion.62 = (bf16[10240,128]{1,0:T(8,128)(2,1)S(1)}, bf16[10240,128]{1,0:T(8,128)(2,1)}) fusion(bf16[10240,256]{1,0:T(8,128)(2,1)} %bitcast.1), kind=kLoop, calls=%fused_computation.91 | loop fusion | bytes 10485760 | tf_op jit(solution)/shard_map/slice | solution.py:76
  234.5 3.8 %gather_fusion = bf16[704,128]{1,0:T(8,128)(2,1)S(1)} fusion(bf16[10240,128]{1,0:T(8,128)(2,1)} %get-tuple-element.10, s32[1024]{0:T(1024)S(1)} %pad_clamp_fusion), kind=kCustom, calls=%fused_computation.clone | custom fusion | bytes 363264 | tf_op jit(solution)/shard_map/jit(_take)/gather | solution.py:122
  238.3 2.0 gather_fusion.1
  240.3 1.0 select_select_fusion
  241.3 77.8 %all-reduce.2.cloned.1.call-done = bf16[320,8192]{1,0:T(8,128)(2,1)} async-done(((bf16[320,8192]{1,0:T(8,128)(2,1)}), bf16[320,8192]{1,0:T(8,128)(2,1)}) %all-reduce.2.cloned.1.call-update) | async-done | bytes 5242896 | tf_op jit(solution)/shard_map/psum | solution.py:110
  319.1 6.0 %multiply_reduce_fusion = f32[320]{0:T(512)S(1)} fusion(bf16[320,8192]{1,0:T(8,128)(2,1)} %all-reduce.2.cloned.1.call-done, bf16[320,8192]{1,0:T(8,128)(2,1)} %param.13), kind=kLoop, calls=%fused_computation.13 | loop fusion | flops 13106880 | bytes 10487040 | tf_op jit(solution)/shard_map/reduce_sum | solution.py:112
  325.1 0.0 copy-done.2
  325.1 7.1 %multiply_convert_fusion = bf16[320,8192]{1,0:T(8,128)(2,1)} fusion(bf16[320,8192]{1,0:T(8,128)(2,1)S(1)} %copy-done.2, bf16[320,8192]{1,0:T(8,128)(2,1)} %param.13, f32[8192]{0:T(1024)S(1)} %convert_element_type.52, f32[320]{0:T(512)S(1)} %add_rsqrt_fusion), kind=kLoop, calls=%fused_computation.12 | loop fusion | flops 15728640 | bytes 15762688 | tf_op jit(solution)/shard_map/convert_element_type | solution.py:113
  (22 shorter events, 0.2 us)
Async XLA Ops:
  7.2 145.7 %copy-start = (bf16[320,512]{1,0:T(8,128)(2,1)S(1)}, bf16[320,512]{1,0:T(8,128)(2,1)}, u32[]{:S(2)}) copy-start(bf16[320,512]{1,0:T(8,128)(2,1)} %param.9) | copy-start | bytes 983044
  7.2 16.7 %copy-start.4 = (s32[18]{0:T(128)S(1)}, s32[18]{0:T(128)}, u32[]{:S(2)}) copy-start(s32[18]{0:T(128)} %param.15) | copy-start | bytes 220
  7.2 17.0 %copy-start.3 = (bf16[8192]{0:T(1024)(128)(2,1)S(1)}, bf16[8192]{0:T(1024)(128)(2,1)}, u32[]{:S(2)}) copy-start(bf16[8192]{0:T(1024)(128)(2,1)} %param.14) | copy-start | bytes 49156
  11.1 141.7 %all-to-all-start = ((bf16[32,320,256]{2,1,0:T(8,128)(2,1)}), bf16[32,320,256]{2,1,0:T(8,128)(2,1)}, u32[]{:S(2)}, u32[]{:S(2)}) async-start(bf16[32,320,256]{2,1,0:T(8,128)(2,1)} %stack.2), calls=%async_computation | async-start | bytes 10485760 | tf_op jit(solution)/shard_map/all_to_all | solution.py:67
  23.1 199.4 %all-gather.2.cloned.1.call-start = ((), (), s32[]{:S(2)}) async-start(), calls=%async_computation.1 | async-start | bytes 8650752 | tf_op jit(solution)/shard_map/all_gather | solution.py:107
  23.9 295.2 %all-reduce.2.cloned.1.call-start = ((), (), s32[]{:S(2)}) async-start(), calls=%async_computation.2 | async-start | bytes 10485760 | tf_op jit(solution)/shard_map/psum | solution.py:110
  319.1 6.0 %copy-start.2 = (bf16[320,8192]{1,0:T(8,128)(2,1)S(1)}, bf16[320,8192]{1,0:T(8,128)(2,1)}, u32[]{:S(2)}) copy-start(bf16[320,8192]{1,0:T(8,128)(2,1)} %all-reduce.2.cloned.1.call-done) | copy-start | bytes 15728644
  319.1 13.1 %copy-start.1 = (bf16[320,512]{1,0:T(8,128)(2,1)S(1)}, bf16[320,512]{1,0:T(8,128)(2,1)}, u32[]{:S(2)}) copy-start(bf16[320,512]{1,0:T(8,128)(2,1)} %param.9) | copy-start | bytes 983044
Sparse Core Ops, SparseCore 0:
  26.4 169.8 all-gather.1
  230.9 88.2 all-reduce.1
